TPU v7x, 32 devices: a whole 2x2x4 slice. The times are simulated.
32 devices in a mesh: grp: 2 (over x), row: 16 (over z, y, core).
Axes of the slice: x: 2, y: 2, z: 4, core: 2. Of those that a mesh axis runs over, the one named last changes fastest.
Arguments:
- panels: bfloat16 [3, 8192, 1536], P(None, 'row'), may hold values from -0.099436891 to 0.099436891, as said below
- first_f: bfloat16 [1536, 512], P('row', 'grp'), parts along dimension 1, may hold values from -6 to 6
- first_g: bfloat16 [1536, 512], P('row', 'grp'), parts along dimension 1, may hold values from -6 to 6
- phase: float32 [4, 1536], P('grp'), parts along dimension 0, may hold values from -3.140625 to 3.140625
- wavenum: float32 [4, 1536], P('grp'), parts along dimension 0, may hold values from 0.5 to 2
Outputs:
- final_f: float32 [1536, 512], P('row', 'grp'), parts along dimension 1
- final_g: float32 [1536, 512], P('row', 'grp'), parts along dimension 1
There are 2 independent parts, one for each index of `grp`. A program takes and returns all parts, laid end to end along the dimension named above; an argument that names none is the same for every part. Nothing has to cross between parts.
Inputs may be any that keep to these rules, and one draw needn't show every extreme that they name: `panels`: consecutive sectors' surface functions share part of their shape.
All inputs are finite; a program needn't handle non-finite values.
Results may differ from a plain program's by a relative error of at most 0.013.
Values may be sent and summed in bfloat16 or wider, within the bound.
No kernel may reach another device: no remote copies, remote signals or barrier semaphores. Data moves between devices by JAX's collectives and lax.ppermute only.
A program may use at most 64 MiB of HBM per device.

v0:
```python
import jax
import jax.numpy as jnp
from jax import lax
from jax.sharding import PartitionSpec as P

SECTORS = 2


def contract_rows(left, right):
    return lax.dot_general(
        left, right, (((0,), (0,)), ((), ())), preferred_element_type=jnp.float32
    )


def shards(panels, first_f, first_g, phase, wavenum):
    chan_rows = first_f.shape[0]
    width = first_f.shape[1]
    all_channels = chan_rows * lax.axis_size("row")
    first_row = lax.axis_index("row") * chan_rows
    solutions = lax.all_gather(
        jnp.concatenate([first_f, first_g], axis=1), "row", axis=0, tiled=True
    )
    for sector in range(SECTORS):
        projected = jnp.dot(panels[sector], solutions, preferred_element_type=jnp.float32).astype(
            jnp.bfloat16
        )
        rotated = lax.psum(contract_rows(panels[sector + 1], projected), "row")
        rot_amp = rotated[:, :width]
        rot_der = rotated[:, width:]
        cosine = jnp.cos(phase[sector])[:, None]
        sine = jnp.sin(phase[sector])[:, None]
        wave = wavenum[sector][:, None]
        new_amp = cosine * rot_amp + sine / wave * rot_der
        new_der = -wave * sine * rot_amp + cosine * rot_der
        norm = jnp.sum(new_amp * new_amp, axis=0) + jnp.sum(new_der * new_der, axis=0)
        scale = 1.0 / jnp.sqrt(norm / (2.0 * all_channels) + 1e-06)
        amp = new_amp * scale[None, :]
        der = new_der * scale[None, :]
        solutions = jnp.concatenate([amp, der], axis=1).astype(jnp.bfloat16)
    amp = lax.dynamic_slice_in_dim(amp, first_row, chan_rows, 0)
    der = lax.dynamic_slice_in_dim(der, first_row, chan_rows, 0)
    return (amp, der)


def solution(mesh):
    in_specs = (
        P(None, "row", None),
        P("row", "grp"),
        P("row", "grp"),
        P("grp", None),
        P("grp", None),
    )
    out_specs = (P("row", "grp"), P("row", "grp"))
    return jax.shard_map(shards, mesh=mesh, in_specs=in_specs, out_specs=out_specs, check_vma=False)
```

profile of v0, /device:TPU:0, one launch (start us, length us, event | category | flops | bytes accessed | tf_op | source)
XLA Modules:
  0.0 283.9 jit_solution(17807892676333385672)
XLA Ops:
  7.2 0.0 all-gather.2.cloned.1.call-start
  7.2 1.5 pad_maximum_fusion
  8.7 0.0 all-gather.2.cloned.1.call-update
  8.7 0.0 all-reduce.3.cloned.1.call-start
  8.8 44.5 %all-gather.2.cloned.1.call-done = bf16[1536,512]{1,0:T(8,128)(2,1)} async-done(((bf16[96,512]{1,0:T(8,128)(2,1)}), bf16[1536,512]{1,0:T(8,128)(2,1)}) %all-gather.2.cloned.1.call-update) | async-done | bytes 1572880 | tf_op jit(solution)/shard_map/all_gather | solution.py:20
  53.3 5.9 %convolution_bitcast_fusion.1 = f32[1536,512]{0,1:T(8,128)} fusion(bf16[3,512,1536]{2,1,0:T(8,128)(2,1)} %param.5, bf16[1536,512]{1,0:T(8,128)(2,1)} %all-gather.2.cloned.1.call-done), kind=kOutput, calls=%fused_computation.1 | convolution fusion | flops 1610874880 | bytes 7864320 | tf_op jit(solution)/shard_map/dot_general | solution.py:10
  59.1 0.0 copy-start.1
  59.1 0.0 copy-start.2
  59.1 0.0 all-reduce.3.cloned.1.call-update
  59.2 0.0 all-reduce.5.cloned.1.call-start
  59.2 0.6 copy-done.1
  59.9 0.0 copy-done.2
  59.9 0.4 cosine_reduce_fusion.1
  60.3 101.2 %all-reduce.3.cloned.1.call-done = f32[1536,512]{0,1:T(8,128)} async-done(((f32[1536,512]{0,1:T(8,128)}), f32[1536,512]{0,1:T(8,128)}) %all-reduce.3.cloned.1.call-update) | async-done | bytes 3145744 | tf_op jit(solution)/shard_map/psum | solution.py:27
  161.5 0.0 copy-start
  161.5 2.7 multiply_reduce_fusion.2
  164.2 0.2 copy-done
  164.3 0.5 multiply_convert_fusion.1
  164.9 5.4 %convolution_bitcast_fusion = f32[1536,512]{0,1:T(8,128)} fusion(bf16[3,512,1536]{2,1,0:T(8,128)(2,1)} %param.5, bf16[1536,256]{0,1:T(8,128)(2,1)S(1)} %get-tuple-element.17, bf16[1536,256]{0,1:T(8,128)(2,1)S(1)} %get-tuple-element.16), kind=kOutput, calls=%fused_computation | convolution fusion | flops 1614020608 | bytes 7864320 | tf_op jit(solution)/shard_map/dot_general | solution.py:10
  170.3 0.0 all-reduce.5.cloned.1.call-update
  170.3 102.9 %all-reduce.5.cloned.1.call-done = f32[1536,512]{0,1:T(8,128)} async-done(((f32[1536,512]{0,1:T(8,128)}), f32[1536,512]{0,1:T(8,128)}) %all-reduce.5.cloned.1.call-update) | async-done | bytes 3145744 | tf_op jit(solution)/shard_map/psum | solution.py:27
  273.2 2.5 multiply_reduce_fusion
  275.7 0.2 dynamic-slice_multiply_fusion
  275.9 0.7 copy.7
  276.6 0.7 copy.8
  (5 shorter events, 0.1 us)
Async XLA Ops:
  7.2 46.1 %all-gather.2.cloned.1.call-start = ((), (), s32[]{:S(2)}) async-start(), calls=%async_computation | async-start | bytes 1671168 | tf_op jit(solution)/shard_map/all_gather | solution.py:20
  8.7 152.8 %all-reduce.3.cloned.1.call-start = ((), (), s32[]{:S(2)}) async-start(), calls=%async_computation.1 | async-start | bytes 6291456 | tf_op jit(solution)/shard_map/psum | solution.py:27
  59.1 0.7 copy-start.1
  59.1 0.7 copy-start.2
  59.2 214.0 %all-reduce.5.cloned.1.call-start = ((), (), s32[]{:S(2)}) async-start(), calls=%async_computation.2 | async-start | bytes 6291456 | tf_op jit(solution)/shard_map/psum | solution.py:27
  161.5 2.8 copy-start
Sparse Core Ops, SparseCore 0:
  10.9 42.3 all-gather.1
  59.3 102.1 all-reduce.2
  170.4 102.7 all-reduce.4
where the time goes:
time: 284 us
  waiting for transfers between devices  249 us (88%)
  between operations  13.8 us (5%)
  matrix products  11.3 us (4%)
  other arithmetic  7.44 us (3%)
    psum x2, waiting for transfers between devices, shards(): rotated = lax.psum(contract_rows(panels[sector + 1], projected), 'row')  204 us
    all_gather x1, waiting for transfers between devices, shards(): lax.all_gather(jnp.concatenate([first_f, first_g], axis=1), 'row', axis=0...  44.5 us
    dot_general x2, matrix products, contract_rows(): lax.dot_general(left, right, (((0,), (0,)), ((), ())), preferred_element_...  11.3 us
  transfers between devices with their start and end apart: 3, of which 3 were waited for; matrix products, arithmetic and copies ran while one was open for 0% of the time, Pallas kernels for 0%

commit v1 on v0

--- a/solution.py
+++ b/solution.py
@@ -4,6 +4,18 @@
 from jax.sharding import PartitionSpec as P
 
 SECTORS = 2
+
+
+def collect(array, axis, dim):
+    ways, here = (lax.axis_size(axis), lax.axis_index(axis))
+    grown, reach = (array, 1)
+    while reach < ways:
+        theirs = lax.ppermute(grown, axis, [(d, d ^ reach) for d in range(ways)])
+        mine_first = jnp.concatenate([grown, theirs], axis=dim)
+        theirs_first = jnp.concatenate([theirs, grown], axis=dim)
+        grown = jnp.where(here & reach == 0, mine_first, theirs_first)
+        reach = 2 * reach
+    return grown
 
 
 def contract_rows(left, right):
@@ -17,9 +29,7 @@
     width = first_f.shape[1]
     all_channels = chan_rows * lax.axis_size("row")
     first_row = lax.axis_index("row") * chan_rows
-    solutions = lax.all_gather(
-        jnp.concatenate([first_f, first_g], axis=1), "row", axis=0, tiled=True
-    )
+    solutions = collect(jnp.concatenate([first_f, first_g], axis=1), "row", 0)
     for sector in range(SECTORS):
         projected = jnp.dot(panels[sector], solutions, preferred_element_type=jnp.float32).astype(
             jnp.bfloat16

time: 284 us -> 298 us (1.049)
  starting transfers between devices: 0.12 us -> 7.89 us
  waiting for transfers between devices: 249 us -> 254 us
    ppermute x0 -> x4, waiting for transfers between devices: none -> 48.5 us  [collect(): theirs = lax.ppermute(grown, axis, [(d, d ^ reach) for d in range(ways)])]
    all_gather x1 -> x0, waiting for transfers between devices: 44.5 us -> none  [shards(): lax.all_gather(jnp.concatenate([first_f, first_g], axis=1), 'row', axis=0...]
    ppermute x0 -> x4, starting transfers between devices: none -> 7.81 us  [collect(): theirs = lax.ppermute(grown, axis, [(d, d ^ reach) for d in range(ways)])]
  transfers between devices with their start and end apart: 3 -> 6, of which waited for: 3 -> 6; matrix products, arithmetic and copies ran while one was open for 0% -> 0% of each run, Pallas kernels for 0% -> 0%
where the time goes in v1:
time: 298 us
  waiting for transfers between devices  254 us (85%)
  between operations  14.1 us (5%)
  matrix products  10.8 us (4%)
  starting transfers between devices  7.89 us (3%)
  other arithmetic  6.44 us (2%)
  local copies, waits for them, and re-layouts  4.29 us (1%)
    psum x2, waiting for transfers between devices, shards(): rotated = lax.psum(contract_rows(panels[sector + 1], projected), 'row')  206 us
    ppermute x4, waiting for transfers between devices, collect(): theirs = lax.ppermute(grown, axis, [(d, d ^ reach) for d in range(ways)])  48.5 us
    dot_general x2, matrix products, contract_rows(): lax.dot_general(left, right, (((0,), (0,)), ((), ())), preferred_element_...  10.8 us
    ppermute x4, starting transfers between devices, collect(): theirs = lax.ppermute(grown, axis, [(d, d ^ reach) for d in range(ways)])  7.81 us
  transfers between devices with their start and end apart: 6, of which 6 were waited for; matrix products, arithmetic and copies ran while one was open for 0% of the time, Pallas kernels for 0%

profile of v1, /device:TPU:0, one launch (start us, length us, event | category | flops | bytes accessed | tf_op | source)
XLA Modules:
  0.0 297.9 jit_solution(16058147836180715863)
XLA Ops:
  7.2 0.0 all-reduce.3.cloned.1.call-start
  7.2 0.8 constant_dynamic-update-slice_fusion.1
  8.0 0.8 constant_dynamic-update-slice_fusion
  8.8 0.5 collective-permute-start
  9.3 0.9 collective-permute-done
  10.3 2.9 collective-permute-start.1
  13.2 5.2 %collective-permute-done.1 = bf16[192,512]{1,0:T(8,128)(2,1)S(1)} collective-permute-done((bf16[192,512]{1,0:T(8,128)(2,1)S(1)}, bf16[192,512]{1,0:T(8,128)(2,1)S(1)}, u32[]{:S(2)}, u32[]{:S(2)}) %collective-permute-start.1) | collective-permute-done | bytes 196640 | tf_op jit(solution)/shard_map/ppermute | solution.py:13
  18.4 0.1 maximum_select_fusion.7
  18.5 1.9 collective-permute-start.2
  20.4 8.9 %collective-permute-done.2 = bf16[384,512]{1,0:T(8,128)(2,1)S(1)} collective-permute-done((bf16[384,512]{1,0:T(8,128)(2,1)S(1)}, bf16[384,512]{1,0:T(8,128)(2,1)S(1)}, u32[]{:S(2)}, u32[]{:S(2)}) %collective-permute-start.2) | collective-permute-done | bytes 393248 | tf_op jit(solution)/shard_map/ppermute | solution.py:13
  29.3 0.3 maximum_select_fusion.6
  29.6 2.6 collective-permute-start.3
  32.1 33.5 %collective-permute-done.3 = bf16[768,512]{1,0:T(8,128)(2,1)S(1)} collective-permute-done((bf16[768,512]{1,0:T(8,128)(2,1)S(1)}, bf16[768,512]{1,0:T(8,128)(2,1)S(1)}, u32[]{:S(2)}, u32[]{:S(2)}) %collective-permute-start.3) | collective-permute-done | bytes 786464 | tf_op jit(solution)/shard_map/ppermute | solution.py:13
  65.6 5.4 %convolution_bitcast_fusion.1 = f32[1536,512]{0,1:T(8,128)} fusion(bf16[3,512,1536]{2,1,0:T(8,128)(2,1)} %param.5, bf16[768,512]{1,0:T(8,128)(2,1)S(1)} %collective-permute-done.3, bf16[768,512]{1,0:T(8,128)(2,1)S(1)} %maximum_select_fusion.6, pred[]{:T(512)S(6)} %eq.12), kind=kOutput, calls=%fused_computation.1 | convolution fusion | flops 1617952768 | bytes 7864321 | tf_op jit(solution)/shard_map/dot_general | solution.py:22
  71.0 0.0 copy-start.1
  71.0 0.0 copy-start.2
  71.0 0.0 all-reduce.3.cloned.1.call-update
  71.0 0.0 all-reduce.5.cloned.1.call-start
  71.1 0.6 copy-done.1
  71.8 0.0 copy-done.2
  71.8 0.4 cosine_reduce_fusion.1
  72.2 103.1 %all-reduce.3.cloned.1.call-done = f32[1536,512]{0,1:T(8,128)} async-done(((f32[1536,512]{0,1:T(8,128)}), f32[1536,512]{0,1:T(8,128)}) %all-reduce.3.cloned.1.call-update) | async-done | bytes 3145744 | tf_op jit(solution)/shard_map/psum | solution.py:37
  175.3 0.0 copy-start
  175.3 2.7 multiply_reduce_fusion.2
  178.0 0.2 copy-done
  178.1 0.5 multiply_convert_fusion.1
  178.7 5.4 %convolution_bitcast_fusion = f32[1536,512]{0,1:T(8,128)} fusion(bf16[3,512,1536]{2,1,0:T(8,128)(2,1)} %param.5, bf16[1536,256]{0,1:T(8,128)(2,1)S(1)} %get-tuple-element.17, bf16[1536,256]{0,1:T(8,128)(2,1)S(1)} %get-tuple-element.16), kind=kOutput, calls=%fused_computation | convolution fusion | flops 1614020608 | bytes 7864320 | tf_op jit(solution)/shard_map/dot_general | solution.py:22
  184.1 0.0 all-reduce.5.cloned.1.call-update
  184.1 102.7 %all-reduce.5.cloned.1.call-done = f32[1536,512]{0,1:T(8,128)} async-done(((f32[1536,512]{0,1:T(8,128)}), f32[1536,512]{0,1:T(8,128)}) %all-reduce.5.cloned.1.call-update) | async-done | bytes 3145744 | tf_op jit(solution)/shard_map/psum | solution.py:37
  286.8 2.5 multiply_reduce_fusion
  289.4 0.2 dynamic-slice_multiply_fusion
  289.6 0.7 copy.7
  290.3 0.7 copy.8
  (6 shorter events, 0.1 us)
Async XLA Ops:
  7.2 168.1 %all-reduce.3.cloned.1.call-start = ((), (), s32[]{:S(2)}) async-start(), calls=%async_computation | async-start | bytes 6291456 | tf_op jit(solution)/shard_map/psum | solution.py:37
  8.8 1.4 collective-permute-start
  10.3 8.2 %collective-permute-start.1 = (bf16[192,512]{1,0:T(8,128)(2,1)S(1)}, bf16[192,512]{1,0:T(8,128)(2,1)S(1)}, u32[]{:S(2)}, u32[]{:S(2)}) collective-permute-start(bf16[192,512]{1,0:T(8,128)(2,1)S(1)} %maximum_select_fusion.8), channel_id=1, source_target_pairs={{0,2},{1,3},{2,0},{3,1},{4,6},{5,7},{6,4},{7,5},{8,10},{9,11},{10,... | collective-permute-start | bytes 589832 | tf_op jit(solution)/shard_map/ppermute | solution.py:13
  18.5 10.7 %collective-permute-start.2 = (bf16[384,512]{1,0:T(8,128)(2,1)S(1)}, bf16[384,512]{1,0:T(8,128)(2,1)S(1)}, u32[]{:S(2)}, u32[]{:S(2)}) collective-permute-start(bf16[384,512]{1,0:T(8,128)(2,1)S(1)} %maximum_select_fusion.7), channel_id=1, source_target_pairs={{0,4},{1,5},{2,6},{3,7},{4,0},{5,1},{6,2},{7,3},{8,12},{9,13},{10,... | collective-permute-start | bytes 1179656 | tf_op jit(solution)/shard_map/ppermute | solution.py:13
  29.6 36.0 %collective-permute-start.3 = (bf16[768,512]{1,0:T(8,128)(2,1)S(1)}, bf16[768,512]{1,0:T(8,128)(2,1)S(1)}, u32[]{:S(2)}, u32[]{:S(2)}) collective-permute-start(bf16[768,512]{1,0:T(8,128)(2,1)S(1)} %maximum_select_fusion.6), channel_id=1, source_target_pairs={{0,8},{1,9},{2,10},{3,11},{4,12},{5,13},{6,14},{7,15},{8,0},{9,1},... | collective-permute-start | bytes 2359304 | tf_op jit(solution)/shard_map/ppermute | solution.py:13
  71.0 0.7 copy-start.1
  71.0 0.7 copy-start.2
  71.0 215.8 %all-reduce.5.cloned.1.call-start = ((), (), s32[]{:S(2)}) async-start(), calls=%async_computation.1 | async-start | bytes 6291456 | tf_op jit(solution)/shard_map/psum | solution.py:37
  175.3 2.8 copy-start
Sparse Core Ops, SparseCore 0:
  71.2 104.0 all-reduce.2
  184.2 102.5 all-reduce.4
